TPU v7x, 256 devices: a whole 4x4x8 slice. The times are simulated.
256 devices in a mesh: sn: 64 (over y, z, core), rhs: 4 (over x).
Axes of the slice: x: 4, y: 4, z: 8, core: 2. Of those that a mesh axis runs over, the one named last changes fastest.
Arguments:
- leaf_rhs: float32 [256, 1024, 256], P('rhs', 'sn'), may hold values from -6 to 6
- root_rhs: float32 [256, 4096], P('rhs', 'sn'), may hold values from -6 to 6
- leaf_inverse: float32 [1024, 256, 256], P('sn'), as said below
- leaf_offdiagonal_block: float32 [1024, 128, 256], P('sn'), may hold values from -0.125 to 0.125
- update_rows: int32 [1024, 128], P('sn'), may hold values from 0 to 4095, as said below
- leaf_sizes: int32 [1024], P('sn'), may hold values from 1 to 256, 163840 in all
- root_inverse: float32 [4096, 4096], P('sn', 'rhs'), as said below
Outputs:
- leaf_solution: float32 [256, 1024, 256], P('rhs', 'sn')
- root_solution: float32 [256, 4096], P('rhs', 'sn')
Inputs may be any that keep to these rules, and one draw needn't show every extreme that they name: `update_rows`: the 128 rows of one leaf are distinct. `leaf_inverse`: lower triangular with a positive diagonal. `root_inverse`: lower triangular with a positive diagonal.
All inputs are finite; a program needn't handle non-finite values. No bound on the sum of `leaf_sizes` on one device may be relied on, other than what follows from the above.
Results may differ from a plain program's by a relative error of at most 0.00015.
Values sent between devices are 32-bit elements; how exact they have to be, the bound alone decides.
No kernel may reach another device: no remote copies, remote signals or barrier semaphores. Data moves between devices by JAX's collectives and lax.ppermute only.
A program may use at most 64 MiB of HBM per device.

v0:
```python
import jax
import jax.numpy as jnp
from jax import lax
from jax.sharding import PartitionSpec as P


def on_device(
    leaf_rhs, root_rhs, leaf_inverse, leaf_offdiagonal_block, update_rows, leaf_sizes, root_inverse
):
    largest_entry = lax.Precision.HIGHEST
    leaf_count = leaf_inverse.shape[0]
    leaf_width = leaf_inverse.shape[1]
    touched = leaf_offdiagonal_block.shape[1]
    columns = leaf_rhs.shape[0]
    slot_index = lax.broadcasted_iota(jnp.int32, (leaf_count, leaf_width), 1)
    live_mask = (slot_index < leaf_sizes[:, None]).astype(jnp.float32)
    masked = leaf_inverse * live_mask[:, :, None] * live_mask[:, None, :]
    leaf_forward_sweep = jnp.einsum("clt,lst->cls", leaf_rhs, masked, precision=largest_entry)
    update_terms = jnp.einsum(
        "dwu,wqu->dwq", leaf_forward_sweep, leaf_offdiagonal_block, precision=largest_entry
    )
    root_full = lax.all_gather(root_inverse, "rhs", axis=1, tiled=True)
    root_order = root_full.shape[1]
    flat_rows = update_rows.reshape(-1)
    accumulated_sum = (
        jnp.zeros((columns, root_order), jnp.float32)
        .at[:, flat_rows]
        .add(update_terms.reshape(columns, leaf_count * touched))
    )
    shares = lax.psum_scatter(accumulated_sum, "sn", scatter_dimension=1, tiled=True)
    reduced = root_rhs - shares
    forward_root = jnp.einsum(
        "cj,ij->ci",
        lax.all_gather(reduced, "sn", axis=1, tiled=True),
        root_full,
        precision=largest_entry,
    )
    back_terms = jnp.einsum("ci,ij->cj", forward_root, root_full, precision=largest_entry)
    root_solution = lax.psum_scatter(back_terms, "sn", scatter_dimension=1, tiled=True)
    root_values = lax.all_gather(root_solution, "sn", axis=1, tiled=True)
    selected_rows = jnp.take(root_values, flat_rows, axis=1).reshape(columns, leaf_count, touched)
    adjusted_values = leaf_forward_sweep - jnp.einsum(
        "rnv,nvb->rnb", selected_rows, leaf_offdiagonal_block, precision=largest_entry
    )
    leaf_solution = jnp.einsum("cls,lst->clt", adjusted_values, masked, precision=largest_entry)
    return (leaf_solution, root_solution)


def solution(mesh):
    in_specs = (
        P("rhs", "sn", None),
        P("rhs", "sn"),
        P("sn", None, None),
        P("sn", None, None),
        P("sn", None),
        P("sn"),
        P("sn", "rhs"),
    )
    out_specs = (P("rhs", "sn", None), P("rhs", "sn"))
    return jax.shard_map(
        on_device, mesh=mesh, in_specs=in_specs, out_specs=out_specs, check_vma=False
    )
```

profile of v0, /device:TPU:1, one launch (start us, length us, event | category | flops | bytes accessed | tf_op | source)
XLA Modules:
  0.0 512.4 jit_solution(12175633617764443415)
XLA Ops:
  8.0 0.0 copy-start
  8.0 0.0 reduce-scatter.5.cloned.1.call-start
  8.1 0.9 fusion.15
  8.9 7.4 %fusion.6 = f32[64,16,256]{2,0,1:T(8,128)S(1)} fusion(f32[16,256,256]{2,1,0:T(8,128)} %param.9, f32[16,256]{1,0:T(8,128)S(1)} %fusion.15, f32[64,16,256]{2,1,0:T(8,128)} %param.7), kind=kOutput, calls=%fused_computation.11 | convolution fusion | flops 807403520 | bytes 6307840 | tf_op jit(solution)/shard_map/clt,lst->cls/dot_general | solution.py:18
  16.3 0.0 copy-done
  16.3 2.3 convolution_bitcast_fusion.2
  18.6 0.0 copy-start.3
  18.6 0.8 copy.32
  19.4 2.4 copy.21
  21.8 0.0 copy-done.3
  21.8 0.0 copy-start.4
  21.8 13.2 %scatter_custom_fusion = f32[64,4096]{0,1:T(8,128)} fusion(s32[2048]{0:T(1024)S(1)} %bitcast.38, f32[2048,64]{1,0:T(8,128)} %copy.21, f32[]{:T(128)} %constant.18.clone.1), kind=kCustom, calls=%fused_computation.16 | custom fusion | flops 131072 | bytes 1049088 | tf_op jit(solution)/shard_map/scatter-add | solution.py:28
  35.1 0.0 reduce-scatter.5.cloned.1.call-update
  35.1 0.0 all-gather.6.cloned.1.call-start
  35.1 0.5 all-gather.6.cloned.1.call-update
  35.7 0.0 all-gather.4.cloned.1.call-start
  35.7 0.0 copy-done.4
  35.7 0.1 copy.22
  35.8 139.6 %reduce-scatter.5.cloned.1.call-done = f32[64,64]{0,1:T(8,128)} async-done(((f32[64,4096]{0,1:T(8,128)}), f32[64,64]{0,1:T(8,128)}) %reduce-scatter.5.cloned.1.call-update) | async-done | bytes 16400 | tf_op jit(solution)/shard_map/reduce_scatter | solution.py:30
  175.4 1.4 sub.6
  176.7 0.0 all-gather.4.cloned.1.call-update
  176.8 0.2 reduce-scatter.7.cloned.1.call-start
  177.0 0.0 all-gather.6.cloned.1.call-done
  177.0 81.1 %all-gather.4.cloned.1.call-done = f32[64,4096]{0,1:T(8,128)} async-done(((f32[64,64]{0,1:T(8,128)}), f32[64,4096]{0,1:T(8,128)}) %all-gather.4.cloned.1.call-update) | async-done | bytes 1048592 | tf_op jit(solution)/shard_map/all_gather | solution.py:34
  258.2 0.0 copy-start.2
  258.2 5.4 %fusion.17 = f32[64,64]{1,0:T(8,128)S(1)} fusion(f32[64,4096]{0,1:T(8,128)} %all-gather.4.cloned.1.call-done, f32[64,4096]{1,0:T(8,128)} %all-gather.6.cloned.1.call-done), kind=kOutput, calls=%fused_computation.29 | convolution fusion | flops 201326592 | bytes 2113536 | tf_op jit(solution)/shard_map/cj,ij->ci/dot_general | solution.py:32
  263.5 0.0 copy-done.2
  263.5 4.8 convolution_bitcast_fusion
  268.3 0.0 reduce-scatter.7.cloned.1.call-update
  268.3 0.0 all-gather.8.cloned.1.call-start
  268.4 133.5 %reduce-scatter.7.cloned.1.call-done = f32[64,64]{1,0:T(8,128)} async-done(((f32[4096,64]{1,0:T(8,128)}), f32[64,64]{1,0:T(8,128)}) %reduce-scatter.7.cloned.1.call-update) | async-done | bytes 16400
  401.9 0.0 all-gather.8.cloned.1.call-update
  402.0 1.5 copy.27
  403.4 82.8 %all-gather.8.cloned.1.call-done = f32[64,4096]{0,1:T(8,128)} async-done(((f32[64,64]{0,1:T(8,128)}), f32[64,4096]{0,1:T(8,128)}) %all-gather.8.cloned.1.call-update) | async-done | bytes 1048592 | tf_op jit(solution)/shard_map/all_gather | solution.py:40
  486.2 9.2 %gather_fusion = f32[2048,64]{1,0:T(8,128)} fusion(f32[64,4096]{0,1:T(8,128)} %all-gather.8.cloned.1.call-done, s32[2048]{0:T(1024)S(1)} %broadcast_clamp_fusion), kind=kCustom, calls=%fused_computation | custom fusion | bytes 1056768 | tf_op jit(solution)/shard_map/jit(_take)/gather | solution.py:41
  495.4 2.3 copy.24
  497.8 0.0 copy-start.1
  497.8 2.5 fusion.8
  500.3 0.0 copy-done.1
  500.3 3.4 fusion.7
  503.7 1.6 copy.25
  (3 shorter events, 0.0 us)
Async XLA Ops:
  8.0 8.3 %copy-start = (f32[16,128,256]{2,1,0:T(8,128)S(1)}, f32[16,128,256]{2,1,0:T(8,128)}, u32[]{:S(2)}) copy-start(f32[16,128,256]{2,1,0:T(8,128)} %param.10) | copy-start | bytes 6291460
  8.0 167.3 %reduce-scatter.5.cloned.1.call-start = ((), (), s32[]{:S(2)}) async-start(), calls=%async_computation.2 | async-start | bytes 2129920 | tf_op jit(solution)/shard_map/reduce_scatter | solution.py:30
  18.6 3.2 copy-start.3
  21.8 13.9 %copy-start.4 = (f32[64,64]{1,0:T(8,128)S(1)}, f32[64,64]{1,0:T(8,128)}, u32[]{:S(2)}) copy-start(f32[64,64]{1,0:T(8,128)} %param.8) | copy-start | bytes 49156
  35.1 141.9 %all-gather.6.cloned.1.call-start = ((), (), s32[]{:S(2)}) async-start(), calls=%async_computation.4 | async-start | bytes 1310720 | tf_op jit(solution)/shard_map/all_gather | solution.py:22
  35.7 222.5 %all-gather.4.cloned.1.call-start = ((), (), s32[]{:S(2)}) async-start(), calls=%async_computation.3 | async-start | bytes 2129920 | tf_op jit(solution)/shard_map/all_gather | solution.py:34
  176.8 225.2 %reduce-scatter.7.cloned.1.call-start = ((), (), s32[]{:S(2)}) async-start(), calls=%async_computation.6 | async-start | bytes 2129920
  258.2 5.4 %copy-start.2 = (f32[64,4096]{1,0:T(8,128)S(1)}, f32[64,4096]{1,0:T(8,128)}, u32[]{:S(2)}) copy-start(f32[64,4096]{1,0:T(8,128)} %all-gather.6.cloned.1.call-done) | copy-start | bytes 3145732
  268.3 217.9 %all-gather.8.cloned.1.call-start = ((), (), s32[]{:S(2)}) async-start(), calls=%async_computation.5 | async-start | bytes 2129920 | tf_op jit(solution)/shard_map/all_gather | solution.py:40
  497.8 2.5 copy-start.1
Sparse Core Ops, SparseCore 0:
  35.2 140.1 reduce-scatter.4
  268.5 133.4 reduce-scatter.6
  404.7 81.4 all-gather.7
Sparse Core Ops, SparseCore 1:
  37.4 28.2 all-gather.5
  176.8 81.3 all-gather.3
where the time goes:
time: 513 us; the launch traced here: 512 us
  waiting for transfers between devices  438 us (85%)
  matrix products  25.7 us (5%)
  local copies, waits for them, and re-layouts  17.9 us (3%)
  other arithmetic  15.5 us (3%)
  between operations  15.3 us (3%)
    reduce_scatter x1, waiting for transfers between devices, on_device(): lax.psum_scatter(accumulated_sum, 'sn', scatter_dimension=1, tiled=True)  140 us
    unnamed x6, waiting for transfers between devices  134 us
    all_gather x1, waiting for transfers between devices, on_device(): root_values = lax.all_gather(root_solution, 'sn', axis=1, tiled=True)  82.8 us
    all_gather x1, waiting for transfers between devices, on_device(): lax.all_gather(reduced, 'sn', axis=1, tiled=True)  81.1 us
    scatter-add x1, other arithmetic, on_device(): accumulated_sum = jnp.zeros((columns, root_order), jnp.float32).at[:, fla...  13.2 us
    gather x2, local copies, waits for them, and re-layouts, on_device(): jnp.take(root_values, flat_rows, axis=1)  11.5 us
  transfers between devices with their start and end apart: 5, of which 4 were waited for; matrix products, arithmetic and copies ran while one was open for 1% of the time, Pallas kernels for 0%

commit v1 on v0

--- a/solution.py
+++ b/solution.py
@@ -37,7 +37,9 @@
     )
     back_terms = jnp.einsum("ci,ij->cj", forward_root, root_full, precision=largest_entry)
     root_solution = lax.psum_scatter(back_terms, "sn", scatter_dimension=1, tiled=True)
-    root_values = lax.all_gather(root_solution, "sn", axis=1, tiled=True)
+    root_values = jnp.concatenate(
+        lax.all_to_all(jnp.stack([root_solution] * lax.axis_size("sn")), "sn", 0, 0), axis=1
+    )
     selected_rows = jnp.take(root_values, flat_rows, axis=1).reshape(columns, leaf_count, touched)
     adjusted_values = leaf_forward_sweep - jnp.einsum(
         "rnv,nvb->rnb", selected_rows, leaf_offdiagonal_block, precision=largest_entry

time: 513 us -> 485 us (0.945)
  waiting for transfers between devices: 438 us -> 383 us
  starting transfers between devices: 0.39 us -> 13.5 us
  local copies, waits for them, and re-layouts: 17.9 us -> 26.6 us
  other arithmetic: 15.5 us -> 20.8 us
    all_gather x1 -> x0, waiting for transfers between devices: 82.8 us -> none  [on_device(): root_values = lax.all_gather(root_solution, 'sn', axis=1, tiled=True)]
    all_to_all x0 -> x1, waiting for transfers between devices: none -> 27.7 us  [on_device(): lax.all_to_all(jnp.stack([root_solution] * lax.axis_size('sn')), 'sn', 0, 0)]
    all_to_all x0 -> x1, starting transfers between devices: none -> 13.1 us  [on_device(): lax.all_to_all(jnp.stack([root_solution] * lax.axis_size('sn')), 'sn', 0, 0)]
    unnamed x13 -> x18, local copies, waits for them, and re-layouts: 3.14 us -> 11.3 us
    all_to_all x0 -> x1, other arithmetic: none -> 5.32 us  [on_device(): lax.all_to_all(jnp.stack([root_solution] * lax.axis_size('sn')), 'sn', 0, 0)]
    unnamed x6 -> x5, waiting for transfers between devices: 134 us -> 134 us
  transfers between devices with their start and end apart: 5 -> 5, of which waited for: 4 -> 4; matrix products, arithmetic and copies ran while one was open for 1% -> 0% of each run, Pallas kernels for 0% -> 0%
where the time goes in v1:
time: 485 us
  waiting for transfers between devices  383 us (79%)
  local copies, waits for them, and re-layouts  26.6 us (5%)
  matrix products  25.7 us (5%)
  other arithmetic  20.8 us (4%)
  between operations  15.6 us (3%)
  starting transfers between devices  13.5 us (3%)
    reduce_scatter x1, waiting for transfers between devices, on_device(): lax.psum_scatter(accumulated_sum, 'sn', scatter_dimension=1, tiled=True)  140 us
    unnamed x5, waiting for transfers between devices  134 us
    all_gather x1, waiting for transfers between devices, on_device(): lax.all_gather(reduced, 'sn', axis=1, tiled=True)  81.1 us
    all_to_all x1, waiting for transfers between devices, on_device(): lax.all_to_all(jnp.stack([root_solution] * lax.axis_size('sn')), 'sn', 0, 0)  27.7 us
    scatter-add x1, other arithmetic, on_device(): accumulated_sum = jnp.zeros((columns, root_order), jnp.float32).at[:, fla...  13.3 us
    all_to_all x1, starting transfers between devices, on_device(): lax.all_to_all(jnp.stack([root_solution] * lax.axis_size('sn')), 'sn', 0, 0)  13.1 us
    gather x2, local copies, waits for them, and re-layouts, on_device(): jnp.take(root_values, flat_rows, axis=1)  11.6 us
    unnamed x18, local copies, waits for them, and re-layouts  11.3 us
  transfers between devices with their start and end apart: 5, of which 4 were waited for; matrix products, arithmetic and copies ran while one was open for 0% of the time, Pallas kernels for 0%

profile of v1, /device:TPU:1, one launch (start us, length us, event | category | flops | bytes accessed | tf_op | source)
XLA Modules:
  0.0 484.8 jit_solution(8085057431793926604)
XLA Ops:
  8.0 0.0 copy-start
  8.0 0.0 reduce-scatter.5.cloned.1.call-start
  8.1 0.9 fusion.15
  8.9 7.4 %fusion.6 = f32[64,16,256]{2,0,1:T(8,128)S(1)} fusion(f32[16,256,256]{2,1,0:T(8,128)} %param.9, f32[16,256]{1,0:T(8,128)S(1)} %fusion.15, f32[64,16,256]{2,1,0:T(8,128)} %param.7), kind=kOutput, calls=%fused_computation.11 | convolution fusion | flops 807403520 | bytes 6307840 | tf_op jit(solution)/shard_map/clt,lst->cls/dot_general | solution.py:18
  16.3 0.0 copy-done
  16.3 2.3 convolution_bitcast_fusion.2
  18.6 0.0 copy-start.4
  18.6 0.8 copy.32
  19.4 2.4 copy.21
  21.8 0.0 copy-done.4
  21.8 0.0 copy-start.5
  21.8 13.3 %scatter_custom_fusion = f32[64,4096]{0,1:T(8,128)} fusion(s32[2048]{0:T(1024)S(1)} %bitcast.45, f32[2048,64]{1,0:T(8,128)} %copy.21, f32[]{:T(128)} %constant.18.clone.1), kind=kCustom, calls=%fused_computation.16 | custom fusion | flops 131072 | bytes 1049088 | tf_op jit(solution)/shard_map/scatter-add | solution.py:28
  35.1 0.0 reduce-scatter.5.cloned.1.call-update
  35.1 0.0 all-gather.5.cloned.1.call-start
  35.2 0.5 all-gather.5.cloned.1.call-update
  35.7 0.0 all-gather.3.cloned.1.call-start
  35.7 0.0 copy-done.5
  35.7 0.1 copy.22
  35.8 139.6 %reduce-scatter.5.cloned.1.call-done = f32[64,64]{0,1:T(8,128)} async-done(((f32[64,4096]{0,1:T(8,128)}), f32[64,64]{0,1:T(8,128)}) %reduce-scatter.5.cloned.1.call-update) | async-done | bytes 16400 | tf_op jit(solution)/shard_map/reduce_scatter | solution.py:30
  175.4 1.4 sub.6
  176.8 0.0 all-gather.3.cloned.1.call-update
  176.8 0.2 reduce-scatter.7.cloned.1.call-start
  177.0 0.0 all-gather.5.cloned.1.call-done
  177.1 81.1 %all-gather.3.cloned.1.call-done = f32[64,4096]{0,1:T(8,128)} async-done(((f32[64,64]{0,1:T(8,128)}), f32[64,4096]{0,1:T(8,128)}) %all-gather.3.cloned.1.call-update) | async-done | bytes 1048592 | tf_op jit(solution)/shard_map/all_gather | solution.py:34
  258.2 0.0 copy-start.2
  258.2 5.4 %fusion.17 = f32[64,64]{1,0:T(8,128)S(1)} fusion(f32[64,4096]{0,1:T(8,128)} %all-gather.3.cloned.1.call-done, f32[64,4096]{1,0:T(8,128)} %all-gather.5.cloned.1.call-done), kind=kOutput, calls=%fused_computation.30 | convolution fusion | flops 201326592 | bytes 2113536 | tf_op jit(solution)/shard_map/cj,ij->ci/dot_general | solution.py:32
  263.6 0.0 copy-done.2
  263.6 4.8 convolution_bitcast_fusion
  268.4 0.0 reduce-scatter.7.cloned.1.call-update
  268.4 133.6 %reduce-scatter.7.cloned.1.call-done = f32[64,64]{1,0:T(8,128)} async-done(((f32[4096,64]{1,0:T(8,128)}), f32[64,64]{1,0:T(8,128)}) %reduce-scatter.7.cloned.1.call-update) | async-done | bytes 16400
  402.0 2.4 broadcast_bitcast_fusion
  404.3 0.0 copy-start.3
  404.3 3.4 reshape.116
  407.8 13.1 %all-to-all-start = ((f32[64,1,4096]{2,1,0:T(1,128)}), f32[64,1,4096]{2,1,0:T(1,128)}, u32[]{:S(2)}, u32[]{:S(2)}) async-start(f32[64,1,4096]{2,1,0:T(1,128)} %reshape.116), calls=%async_computation.1 | async-start | bytes 2097152 | tf_op jit(solution)/shard_map/all_to_all | solution.py:41
  420.9 0.0 copy-done.3
  420.9 0.7 copy.27
  421.6 27.7 %all-to-all-done = f32[64,1,4096]{2,1,0:T(1,128)} async-done(((f32[64,1,4096]{2,1,0:T(1,128)}), f32[64,1,4096]{2,1,0:T(1,128)}, u32[]{:S(2)}, u32[]{:S(2)}) %all-to-all-start) | async-done | bytes 1048608 | tf_op jit(solution)/shard_map/all_to_all | solution.py:41
  449.3 0.5 broadcast.56
  449.9 5.3 %reduce = f32[64,4096]{1,0:T(8,128)} reduce(f32[64,1,4096]{2,1,0:T(1,128)} %all-to-all-done, f32[]{:T(128)} %broadcast.56), dimensions={1}, to_apply=%all_to_all.3.reduce_sub_computation | reduce | bytes 2097156 | tf_op jit(solution)/shard_map/all_to_all | solution.py:41
  455.2 3.1 reshape.117
  458.3 9.2 %gather_fusion = f32[2048,64]{1,0:T(8,128)} fusion(f32[64,4096]{0,1:T(8,128)} %bitcast.39, s32[2048]{0:T(1024)S(1)} %broadcast_clamp_fusion), kind=kCustom, calls=%fused_computation | custom fusion | bytes 1056768 | tf_op jit(solution)/shard_map/jit(_take)/gather | solution.py:43
  467.5 2.3 copy.24
  469.9 0.0 copy-start.1
  469.9 2.5 fusion.8
  472.4 0.0 copy-done.1
  472.4 3.4 fusion.7
  475.8 1.6 copy.25
  (3 shorter events, 0.0 us)
Async XLA Ops:
  8.0 8.3 %copy-start = (f32[16,128,256]{2,1,0:T(8,128)S(1)}, f32[16,128,256]{2,1,0:T(8,128)}, u32[]{:S(2)}) copy-start(f32[16,128,256]{2,1,0:T(8,128)} %param.10) | copy-start | bytes 6291460
  8.0 167.4 %reduce-scatter.5.cloned.1.call-start = ((), (), s32[]{:S(2)}) async-start(), calls=%async_computation.3 | async-start | bytes 2129920 | tf_op jit(solution)/shard_map/reduce_scatter | solution.py:30
  18.6 3.2 copy-start.4
  21.8 13.9 %copy-start.5 = (f32[64,64]{1,0:T(8,128)S(1)}, f32[64,64]{1,0:T(8,128)}, u32[]{:S(2)}) copy-start(f32[64,64]{1,0:T(8,128)} %param.8) | copy-start | bytes 49156
  35.1 141.9 %all-gather.5.cloned.1.call-start = ((), (), s32[]{:S(2)}) async-start(), calls=%async_computation.5 | async-start | bytes 1310720 | tf_op jit(solution)/shard_map/all_gather | solution.py:22
  35.7 222.5 %all-gather.3.cloned.1.call-start = ((), (), s32[]{:S(2)}) async-start(), calls=%async_computation.4 | async-start | bytes 2129920 | tf_op jit(solution)/shard_map/all_gather | solution.py:34
  176.8 225.2 %reduce-scatter.7.cloned.1.call-start = ((), (), s32[]{:S(2)}) async-start(), calls=%async_computation.6 | async-start | bytes 2129920
  258.2 5.4 %copy-start.2 = (f32[64,4096]{1,0:T(8,128)S(1)}, f32[64,4096]{1,0:T(8,128)}, u32[]{:S(2)}) copy-start(f32[64,4096]{1,0:T(8,128)} %all-gather.5.cloned.1.call-done) | copy-start | bytes 3145732
  404.3 16.6 %copy-start.3 = (f32[64,64]{1,0:T(8,128)S(1)}, f32[64,64]{1,0:T(8,128)}, u32[]{:S(2)}) copy-start(f32[64,64]{1,0:T(8,128)} %reduce-scatter.7.cloned.1.call-done) | copy-start | bytes 49156
  407.8 41.6 %all-to-all-start = ((f32[64,1,4096]{2,1,0:T(1,128)}), f32[64,1,4096]{2,1,0:T(1,128)}, u32[]{:S(2)}, u32[]{:S(2)}) async-start(f32[64,1,4096]{2,1,0:T(1,128)} %reshape.116), calls=%async_computation.1 | async-start | bytes 2097152 | tf_op jit(solution)/shard_map/all_to_all | solution.py:41
  469.9 2.5 copy-start.1
Sparse Core Ops, SparseCore 0:
  35.2 140.1 reduce-scatter.4
  268.5 133.4 reduce-scatter.6
Sparse Core Ops, SparseCore 1:
  37.4 28.2 all-gather.4
  176.9 81.3 all-gather.2
